TPU v7x, 128 devices: a whole 4x4x4 slice. The times are simulated.
128 devices in a mesh: ctx: 16 (over z, y), head: 8 (over x, core).
Axes of the slice: x: 4, y: 4, z: 4, core: 2. Of those that a mesh axis runs over, the one named last changes fastest.
Arguments:
- queries: bfloat16 [32768, 8192], P(('ctx', 'head')), may hold values from -150 to 150
- key_states: bfloat16 [32768, 1024], P(('ctx', 'head')), may hold values from -10 to 10
- value_states: bfloat16 [32768, 1024], P(('ctx', 'head')), may hold values from -6 to 6
- page_ids: int32 [256], replicated, may hold values from 0 to 63, never falling along the last dimension, each value on 1 to 8 neighbouring positions
- ref_group: int32 [256, 4], replicated, may hold values from 0 to 15, all different within a row; in each aligned block of 16 rows (0 to 15, 16 to 31, ...) at most 4 rows name the same one
- ref_slot: int32 [256, 4], replicated, may hold values from 0 to 15
Outputs:
- attended: bfloat16 [32768, 8192], P(('ctx', 'head'))
Inputs may be any that keep to these rules, and one draw needn't show every extreme that they name: `page_ids`: ids never fall; every page has 1 to 8 blocks and one has exactly 8. `ref_group`: a row's 4 values differ; the rows of the 16 blocks of one ctx group name every ctx group exactly 4 times.
All inputs are finite; a program needn't handle non-finite values.
Results may differ from a plain program's by a relative error of at most 0.0042.
Values may be sent and summed in bfloat16 or wider, within the bound.
No kernel may reach another device: no remote copies, remote signals or barrier semaphores. Data moves between devices by JAX's collectives and lax.ppermute only.
A program may use at most 128 MiB of HBM per device.

v0:
```python
import math
import jax
import jax.numpy as jnp
from jax import lax
from jax.sharding import PartitionSpec as P

HD = 128
BLOCK = 128
MAXPAGE = 8


def from_behind(block, axis, distance):
    devices = range(lax.axis_size(axis))
    route = [(i - distance, i) for i in devices if i - distance in devices]
    return lax.ppermute(block, axis, route)


def page_starts(page_ids):
    block_count = page_ids.shape[0]
    position = jnp.arange(block_count, dtype=jnp.int32)
    is_fresh = jnp.concatenate([jnp.ones((1,), dtype=jnp.bool_), page_ids[1:] != page_ids[:-1]])
    return lax.cummax(jnp.where(is_fresh, position, jnp.zeros_like(position)), axis=0)


def allowed_mask(global_block, padded_pages, starts, ref_row, block_size, window):
    nearby = lax.dynamic_slice_in_dim(padded_pages, global_block, window, 0)
    own_page = nearby[window - 1]
    inside = nearby == own_page
    offsets = jnp.arange(window)
    is_last = offsets == window - 1
    rows_at = jnp.arange(block_size)
    causal = rows_at[None, :] <= rows_at[:, None]
    window_ok = inside[None, :, None] & (
        jnp.logical_not(is_last)[None, :, None] | causal[:, None, :]
    )
    window_ok = window_ok.reshape(block_size, window * block_size)
    start_here = lax.dynamic_index_in_dim(starts, global_block, 0, keepdims=False)
    ref_ok = ref_row < start_here
    ref_ok = jnp.broadcast_to(ref_ok[None, :, None], (block_size, ref_row.shape[0], block_size))
    return jnp.concatenate([window_ok, ref_ok.reshape(block_size, -1)], axis=1)


def attend(query_block, key_set, value_set, allowed):
    score_scale = 1.0 / math.sqrt(query_block.shape[-1])
    scores = (
        jnp.einsum("tgqd,sgd->gqts", query_block, key_set, preferred_element_type=jnp.float32)
        * score_scale
    )
    scores = jnp.where(allowed, scores, -1e30)
    row_max = jnp.max(scores, axis=-1, keepdims=True)
    exp_scores = jnp.where(allowed, jnp.exp(scores - row_max), 0.0)
    totals = jnp.sum(exp_scores, axis=-1)
    weights = exp_scores.astype(jnp.bfloat16)
    mixture = jnp.einsum("gqts,sgd->tgqd", weights, value_set, preferred_element_type=jnp.float32)
    return (mixture / jnp.transpose(totals, (2, 0, 1))[..., None]).astype(jnp.bfloat16)


def shards(queries, key_states, value_states, page_ids, ref_group, ref_slot):
    head_queries, head_keys, head_values = (
        lax.all_to_all(queries, "head", split_axis=1, concat_axis=0, tiled=True),
        lax.all_to_all(key_states, "head", split_axis=1, concat_axis=0, tiled=True),
        lax.all_to_all(value_states, "head", split_axis=1, concat_axis=0, tiled=True),
    )
    group_tokens = head_keys.shape[0]
    key_width = head_keys.shape[1]
    local_heads = key_width // HD
    blocks = group_tokens // BLOCK
    reach = MAXPAGE - 1
    refs_count = ref_group.shape[1]
    key_blocks = head_keys.reshape(blocks, BLOCK, key_width)
    value_blocks = head_values.reshape(blocks, BLOCK, key_width)
    tail_keys, tail_values = from_behind(
        (key_blocks[blocks - reach :], value_blocks[blocks - reach :]), "ctx", 1
    )
    near_keys = jnp.concatenate([tail_keys, key_blocks])
    near_values = jnp.concatenate([tail_values, value_blocks])
    ctx_group = lax.axis_index("ctx")
    first_block = ctx_group * blocks
    own_groups = lax.dynamic_slice_in_dim(ref_group, first_block, blocks, 0)
    own_slots = lax.dynamic_slice_in_dim(ref_slot, first_block, blocks, 0)
    own_rows = own_groups * blocks + own_slots
    whole_keys, whole_values = (
        lax.all_gather(key_blocks, "ctx", axis=0, tiled=True),
        lax.all_gather(value_blocks, "ctx", axis=0, tiled=True),
    )
    flat_rows = own_rows.reshape(-1)
    far_keys = jnp.take(whole_keys, flat_rows, axis=0).reshape(blocks, refs_count, BLOCK, key_width)
    far_values = jnp.take(whole_values, flat_rows, axis=0).reshape(
        blocks, refs_count, BLOCK, key_width
    )
    padded_pages = jnp.concatenate([jnp.full((reach,), -1, dtype=jnp.int32), page_ids])
    starts = page_starts(page_ids)
    group_size = head_queries.shape[1] // key_width
    query_blocks = head_queries.reshape(blocks, BLOCK, local_heads, group_size, HD)

    def one_block(local_block):
        global_block = first_block + local_block
        ref_row = lax.dynamic_index_in_dim(own_rows, local_block, 0, keepdims=False)
        key_set = jnp.concatenate(
            [
                lax.dynamic_slice_in_dim(near_keys, local_block, MAXPAGE, 0),
                lax.dynamic_index_in_dim(far_keys, local_block, 0, keepdims=False),
            ]
        )
        value_set = jnp.concatenate(
            [
                lax.dynamic_slice_in_dim(near_values, local_block, MAXPAGE, 0),
                lax.dynamic_index_in_dim(far_values, local_block, 0, keepdims=False),
            ]
        )
        allowed = allowed_mask(global_block, padded_pages, starts, ref_row, BLOCK, MAXPAGE)
        query_block = lax.dynamic_index_in_dim(query_blocks, local_block, 0, keepdims=False)
        return attend(
            query_block,
            key_set.reshape(-1, local_heads, HD),
            value_set.reshape(-1, local_heads, HD),
            allowed,
        )

    outputs = lax.map(one_block, jnp.arange(blocks, dtype=jnp.int32))
    merged = outputs.reshape(group_tokens, head_queries.shape[1])
    return lax.all_to_all(merged, "head", split_axis=0, concat_axis=1, tiled=True)


def solution(mesh):
    placed = (
        P(("ctx", "head"), None),
        P(("ctx", "head"), None),
        P(("ctx", "head"), None),
        P(),
        P(),
        P(),
    )
    return jax.shard_map(
        shards, mesh=mesh, in_specs=placed, out_specs=P(("ctx", "head"), None), check_vma=False
    )
```

profile of v0, /device:TPU:1, one launch (start us, length us, event | category | flops | bytes accessed | tf_op | source)
XLA Modules:
  0.0 519.4 jit_solution(513064871498028624)
XLA Ops:
  7.7 15.0 %all_to_all.67 = bf16[256,8,128]{2,0,1:T(8,128)(2,1)} all-to-all(bf16[256,8,128]{2,0,1:T(8,128)(2,1)S(1)} %copy_bitcast_fusion.4), channel_id=1, replica_groups=mesh['ctx'=16,'head'=8] {'head'}, dimensions={1} | all-to-all | bytes 1048576 | tf_op jit(solution)/shard_map/all_to_all | solution.py:62
  23.9 13.4 %all_to_all.68 = bf16[256,8,128]{2,0,1:T(8,128)(2,1)} all-to-all(bf16[256,8,128]{2,0,1:T(8,128)(2,1)S(1)} %copy_bitcast_fusion.3), channel_id=1, replica_groups=mesh['ctx'=16,'head'=8] {'head'}, dimensions={1} | all-to-all | bytes 1048576 | tf_op jit(solution)/shard_map/all_to_all | solution.py:61
  37.4 4.8 copy.62
  42.2 5.6 %all-to-all-start.2 = ((bf16[256,8,1024]{2,0,1:T(8,128)(2,1)}), bf16[256,8,1024]{2,0,1:T(8,128)(2,1)}, u32[]{:S(2)}, u32[]{:S(2)}) async-start(bf16[256,8,1024]{2,0,1:T(8,128)(2,1)} %bitcast.164), calls=%async_computation.2 | async-start | bytes 8388608 | tf_op jit(solution)/shard_map/all_to_all | solution.py:60
  49.0 3.2 collective-permute-start
  52.3 3.2 collective-permute-start.1
  58.0 8.6 %collective-permute-done.1 = bf16[7,128,128]{2,1,0:T(8,128)(2,1)S(1)} collective-permute-done((bf16[7,128,128]{2,1,0:T(8,128)(2,1)S(1)}, bf16[7,128,128]{2,1,0:T(8,128)(2,1)S(1)}, u32[]{:S(2)}, u32[]{:S(2)}) %collective-permute-start.1) | collective-permute-done | bytes 229408 | tf_op jit(solution)/shard_map/ppermute | solution.py:15
  67.5 29.1 %all-to-all-done.2 = bf16[256,8,1024]{2,0,1:T(8,128)(2,1)} async-done(((bf16[256,8,1024]{2,0,1:T(8,128)(2,1)}), bf16[256,8,1024]{2,0,1:T(8,128)(2,1)}, u32[]{:S(2)}, u32[]{:S(2)}) %all-to-all-start.2) | async-done | bytes 4194336 | tf_op jit(solution)/shard_map/all_to_all | solution.py:60
  96.6 5.2 %copy.54 = bf16[256,8,8,128]{3,2,1,0:T(8,128)(2,1)} copy(bf16[256,8,8,128]{3,1,2,0:T(8,128)(2,1)} %bitcast.50) | data formatting | bytes 8388608
  101.8 4.3 gather_fusion
  106.1 66.7 %all-gather.5.cloned.1.call-done = bf16[256,128,128]{2,1,0:T(8,128)(2,1)} async-done(((bf16[16,128,128]{2,1,0:T(8,128)(2,1)}), bf16[256,128,128]{2,1,0:T(8,128)(2,1)}) %all-gather.5.cloned.1.call-update) | async-done | bytes 8388624 | tf_op jit(solution)/shard_map/all_gather | solution.py:83
  172.9 5.6 %gather_fusion.1 = bf16[64,128,128]{2,1,0:T(8,128)(2,1)} fusion(bf16[256,128,128]{2,1,0:T(8,128)(2,1)} %all-gather.5.cloned.1.call-done, s32[1024]{0:T(1024)S(1)} %pad_clamp_fusion), kind=kCustom, calls=%fused_computation.1.clone | custom fusion | bytes 4194560 | tf_op jit(solution)/shard_map/jit(_take)/gather | solution.py:87
  178.4 4.0 broadcast_select_fusion
  182.4 256.0 %while.10 = (s32[]{:T(128)}, bf16[16,128,1,8,128]{4,3,1,0,2:T(8,128)(2,1)}, s32[16]{0:T(128)S(1)}, bf16[23,128,128]{2,1,0:T(8,128)(2,1)}, bf16[16,4,128,128]{3,2...) while((s32[]{:T(128)}, ...), condition=%wide.region_5.7_spmd, body=%wide.region_2.6_spmd.sunk | while | flops 826882048 | bytes 26014728 | solution.py:120
  194.3 1.5 fusion.41
  195.8 1.7 fusion.42
  210.3 1.5 fusion.41
  211.8 1.7 fusion.42
  226.3 1.5 fusion.41
  227.8 1.7 fusion.42
  242.3 1.5 fusion.41
  243.8 1.7 fusion.42
  258.3 1.5 fusion.41
  259.8 1.7 fusion.42
  274.3 1.5 fusion.41
  275.8 1.7 fusion.42
  290.3 1.5 fusion.41
  291.8 1.7 fusion.42
  306.3 1.5 fusion.41
  307.8 1.7 fusion.42
  322.3 1.5 fusion.41
  323.8 1.7 fusion.42
  338.3 1.5 fusion.41
  339.8 1.7 fusion.42
  354.3 1.5 fusion.41
  355.8 1.7 fusion.42
  370.3 1.5 fusion.41
  371.8 1.7 fusion.42
  386.3 1.5 fusion.41
  387.8 1.7 fusion.42
  402.3 1.5 fusion.41
  403.8 1.7 fusion.42
  419.8 1.7 fusion.42
  435.8 1.7 fusion.42
  438.4 7.3 %all_to_all.59 = bf16[8,256,1024]{2,1,0:T(8,128)(2,1)} reshape(bf16[16,128,1,8,128]{4,3,1,0,2:T(8,128)(2,1)} %get-tuple-element.68) | data formatting | bytes 8388608 | tf_op jit(solution)/shard_map/all_to_all | solution.py:122
  445.8 54.0 %all_to_all.69 = bf16[8,256,1024]{2,1,0:T(8,128)(2,1)} all-to-all(bf16[8,256,1024]{2,1,0:T(8,128)(2,1)} %all_to_all.59), channel_id=1, replica_groups=mesh['ctx'=16,'head'=8] {'head'}, dimensions={0} | all-to-all | bytes 8388608 | tf_op jit(solution)/shard_map/all_to_all | solution.py:122
  499.7 6.5 %copy.41 = bf16[256,8,1024]{0,2,1:T(8,128)(2,1)} copy(bf16[256,8,1024]{2,0,1:T(8,128)(2,1)} %bitcast.165) | data formatting | bytes 8388608 | tf_op jit(solution)/shard_map/all_to_all | solution.py:122
  506.2 6.4 %copy.42 = bf16[256,8192]{1,0:T(8,128)(2,1)} copy(bf16[256,8192]{0,1:T(8,128)(2,1)} %bitcast.166) | data formatting | bytes 8388608 | tf_op jit(solution)/shard_map/all_to_all | solution.py:122
  (382 shorter events, 152.9 us)
Async XLA Ops:
  6.5 1.0 copy-start
  6.5 95.3 %all-gather.3.cloned.1.call-start = ((), (), s32[]{:S(2)}) async-start(), calls=%async_computation.4 | async-start | bytes 8912896 | tf_op jit(solution)/shard_map/all_gather | solution.py:84
  22.7 150.2 %all-gather.5.cloned.1.call-start = ((), (), s32[]{:S(2)}) async-start(), calls=%async_computation.5 | async-start | bytes 8912896 | tf_op jit(solution)/shard_map/all_gather | solution.py:83
  42.1 5.6 %copy-start.5 = (s32[256,4]{0,1:T(4,128)S(1)}, s32[256,4]{0,1:T(4,128)}, u32[]{:S(2)}) copy-start(s32[256,4]{0,1:T(4,128)} %param.15) | copy-start | bytes 12292
  42.1 5.6 %copy-start.6 = (s32[256,4]{0,1:T(4,128)S(1)}, s32[256,4]{0,1:T(4,128)}, u32[]{:S(2)}) copy-start(s32[256,4]{0,1:T(4,128)} %param.14) | copy-start | bytes 12292
  42.2 6.0 %copy-start.4 = (s32[256]{0:T(256)S(1)}, s32[256]{0:T(256)}, u32[]{:S(2)}) copy-start(s32[256]{0:T(256)} %param.13) | copy-start | bytes 3076
  42.2 6.8 %copy-start.2 = (bf16[256,8,128]{2,0,1:T(8,128)(2,1)S(1)}, bf16[256,8,128]{2,0,1:T(8,128)(2,1)}, u32[]{:S(2)}) copy-start(bf16[256,8,128]{2,0,1:T(8,128)(2,1)} %all_to_all.67) | copy-start | bytes 1572868
  42.2 10.1 %copy-start.3 = (bf16[256,8,128]{2,0,1:T(8,128)(2,1)S(1)}, bf16[256,8,128]{2,0,1:T(8,128)(2,1)}, u32[]{:S(2)}) copy-start(bf16[256,8,128]{2,0,1:T(8,128)(2,1)} %all_to_all.68) | copy-start | bytes 1572868
  42.2 54.4 %all-to-all-start.2 = ((bf16[256,8,1024]{2,0,1:T(8,128)(2,1)}), bf16[256,8,1024]{2,0,1:T(8,128)(2,1)}, u32[]{:S(2)}, u32[]{:S(2)}) async-start(bf16[256,8,1024]{2,0,1:T(8,128)(2,1)} %bitcast.164), calls=%async_computation.2 | async-start | bytes 8388608 | tf_op jit(solution)/shard_map/all_to_all | solution.py:60
  49.0 8.0 %collective-permute-start = (bf16[7,128,128]{2,1,0:T(8,128)(2,1)S(1)}, bf16[7,128,128]{2,1,0:T(8,128)(2,1)S(1)}, u32[]{:S(2)}, u32[]{:S(2)}) collective-permute-start(bf16[7,128,128]{2,1,0:T(8,128)(2,1)S(1)} %slice.32), channel_id=1, source_target_pairs={{0,8},{8,16},{16,24},{24,32},{32,40},{40,48},{48,56},{56,64},{64,7... | collective-permute-start | bytes 688136 | tf_op jit(solution)/shard_map/ppermute | solution.py:15
  52.3 14.3 %collective-permute-start.1 = (bf16[7,128,128]{2,1,0:T(8,128)(2,1)S(1)}, bf16[7,128,128]{2,1,0:T(8,128)(2,1)S(1)}, u32[]{:S(2)}, u32[]{:S(2)}) collective-permute-start(bf16[7,128,128]{2,1,0:T(8,128)(2,1)S(1)} %slice.33), channel_id=1, source_target_pairs={{0,8},{8,16},{16,24},{24,32},{32,40},{40,48},{48,56},{56,64},{64,7... | collective-permute-start | bytes 688136 | tf_op jit(solution)/shard_map/ppermute | solution.py:15
  506.2 6.4 %copy-start.1 = (bf16[256,1024]{1,0:T(8,128)(2,1)S(1)}, bf16[256,1024]{1,0:T(8,128)(2,1)}, u32[]{:S(2)}) copy-start(bf16[256,1024]{1,0:T(8,128)(2,1)} %param.12) | copy-start | bytes 1572868
Sparse Core Ops, SparseCore 0:
  22.8 77.1 all-gather.2
  102.2 70.6 all-gather.4
where the time goes:
time: 523 us; the launch traced here: 519 us
  local copies, waits for them, and re-layouts  139 us (27%)
  waiting for transfers between devices  106 us (20%)
  blocking collectives  82.4 us (16%)
  loops' own time  62.4 us (12%)
  other arithmetic  61.2 us (12%)
  matrix products  43.3 us (8%)
  between operations  13.5 us (3%)
  starting transfers between devices  12.1 us (2%)
    all_gather x1, waiting for transfers between devices, shards(): lax.all_gather(key_blocks, 'ctx', axis=0, tiled=True)  66.7 us
    another operation x1, loops' own time, shards(): outputs = lax.map(one_block, jnp.arange(blocks, dtype=jnp.int32))  62.4 us
    all_to_all x1, blocking collectives, shards(): lax.all_to_all(merged, 'head', split_axis=0, concat_axis=1, tiled=True)  54 us
    all_to_all x1, waiting for transfers between devices, shards(): lax.all_to_all(queries, 'head', split_axis=1, concat_axis=0, tiled=True)  29.1 us
    dot_general x16, matrix products, attend(): jnp.einsum('gqts,sgd->tgqd', weights, value_set, preferred_element_type=j...  26.6 us
    reduce_sum x16, other arithmetic, attend(): totals = jnp.sum(exp_scores, axis=-1)  24.1 us
    all_to_all x3, local copies, waits for them, and re-layouts, shards(): lax.all_to_all(merged, 'head', split_axis=0, concat_axis=1, tiled=True)  20.2 us
    dynamic_slice x16, local copies, waits for them, and re-layouts, one_block(): lax.dynamic_slice_in_dim(near_keys, local_block, MAXPAGE, 0)  17.1 us
  transfers between devices with their start and end apart: 5, of which 4 were waited for; matrix products, arithmetic and copies ran while one was open for 4% of the time, Pallas kernels for 0%

commit v1 on v0

--- a/solution.py
+++ b/solution.py
@@ -56,6 +56,15 @@
 
 
 def shards(queries, key_states, value_states, page_ids, ref_group, ref_slot):
+
+    def _recast_results(incoming_x, dim_i=0):
+        tray = []
+        for _ in range(lax.axis_size("ctx")):
+            tray.append(incoming_x)
+        z = jnp.stack(tray, axis=0)
+        spare = lax.all_to_all(z, split_axis=0, axis_name="ctx", concat_axis=0)
+        return jnp.concatenate(spare, axis=dim_i)
+
     head_queries, head_keys, head_values = (
         lax.all_to_all(queries, "head", split_axis=1, concat_axis=0, tiled=True),
         lax.all_to_all(key_states, "head", split_axis=1, concat_axis=0, tiled=True),
@@ -80,7 +89,7 @@
     own_slots = lax.dynamic_slice_in_dim(ref_slot, first_block, blocks, 0)
     own_rows = own_groups * blocks + own_slots
     whole_keys, whole_values = (
-        lax.all_gather(key_blocks, "ctx", axis=0, tiled=True),
+        _recast_results(key_blocks),
         lax.all_gather(value_blocks, "ctx", axis=0, tiled=True),
     )
     flat_rows = own_rows.reshape(-1)

time: 523 us -> 591 us (1.13)
  the two profiles are of different devices: /device:TPU:1 before, /device:TPU:24 now
where the time goes in v1:
time: 591 us; the launch traced here: 587 us
  local copies, waits for them, and re-layouts  144 us (24%)
  waiting for transfers between devices  126 us (21%)
  blocking collectives  123 us (21%)
  other arithmetic  62.8 us (11%)
  loops' own time  56.3 us (10%)
  matrix products  43.4 us (7%)
  starting transfers between devices  18.6 us (3%)
  between operations  13.5 us (2%)
    ppermute x2, waiting for transfers between devices, from_behind(): return lax.ppermute(block, axis, route)  121 us
    another operation x1, loops' own time, shards(): outputs = lax.map(one_block, jnp.arange(blocks, dtype=jnp.int32))  56.3 us
    all_to_all x1, blocking collectives, shards(): lax.all_to_all(queries, 'head', split_axis=1, concat_axis=0, tiled=True)  54.2 us
    all_to_all x1, blocking collectives, shards(): lax.all_to_all(merged, 'head', split_axis=0, concat_axis=1, tiled=True)  54.1 us
    dot_general x16, matrix products, attend(): jnp.einsum('gqts,sgd->tgqd', weights, value_set, preferred_element_type=j...  26.7 us
    reduce_sum x16, other arithmetic, attend(): totals = jnp.sum(exp_scores, axis=-1)  24.3 us
    all_to_all x3, local copies, waits for them, and re-layouts, shards(): lax.all_to_all(merged, 'head', split_axis=0, concat_axis=1, tiled=True)  20.2 us
    dot_general x16, matrix products, attend(): jnp.einsum('tgqd,sgd->gqts', query_block, key_set, preferred_element_type...  16.7 us
  transfers between devices with their start and end apart: 5, of which 3 were waited for; matrix products, arithmetic and copies ran while one was open for 4% of the time, Pallas kernels for 0%

profile of v1, /device:TPU:24, one launch (start us, length us, event | category | flops | bytes accessed | tf_op | source)
XLA Modules:
  0.0 587.3 jit_solution(1694733631973532810)
XLA Ops:
  7.7 14.6 %all_to_all.72 = bf16[256,8,128]{2,0,1:T(8,128)(2,1)} all-to-all(bf16[256,8,128]{2,0,1:T(8,128)(2,1)S(1)} %copy_bitcast_fusion.4), channel_id=1, replica_groups=mesh['ctx'=16,'head'=8] {'head'}, dimensions={1} | all-to-all | bytes 1048576 | tf_op jit(solution)/shard_map/all_to_all | solution.py:71
  22.3 2.0 copy_bitcast_fusion.3
  24.2 3.5 all-to-all-start.1
  27.7 4.8 copy.62
  32.6 5.4 all-to-all-done.1
  38.0 54.2 %all_to_all.73 = bf16[256,8,1024]{2,0,1:T(8,128)(2,1)} all-to-all(bf16[256,8,1024]{2,0,1:T(8,128)(2,1)} %bitcast.166), channel_id=1, replica_groups=mesh['ctx'=16,'head'=8] {'head'}, dimensions={1} | all-to-all | bytes 8388608 | tf_op jit(solution)/shard_map/all_to_all | solution.py:69
  92.2 5.4 stack.3
  97.5 8.3 %all-to-all-start.2 = ((bf16[16,16,128,128]{3,2,1,0:T(8,128)(2,1)}), bf16[16,16,128,128]{3,2,1,0:T(8,128)(2,1)}, u32[]{:S(2)}, u32[]{:S(2)}) async-start(bf16[16,16,128,128]{3,2,1,0:T(8,128)(2,1)} %stack.3), calls=%async_computation.2 | async-start | bytes 16777216 | tf_op jit(solution)/shard_map/all_to_all | solution.py:65
  107.1 3.4 collective-permute-start
  110.5 3.4 collective-permute-start.1
  113.9 118.6 %collective-permute-done = bf16[7,128,128]{2,1,0:T(8,128)(2,1)S(1)} collective-permute-done((bf16[7,128,128]{2,1,0:T(8,128)(2,1)S(1)}, bf16[7,128,128]{2,1,0:T(8,128)(2,1)S(1)}, u32[]{:S(2)}, u32[]{:S(2)}) %collective-permute-start) | collective-permute-done | bytes 229408 | tf_op jit(solution)/shard_map/ppermute | solution.py:15
  233.4 2.3 collective-permute-done.1
  235.8 5.2 copy.54
  241.0 4.3 gather_fusion.1
  245.4 5.5 gather_fusion
  250.9 4.0 broadcast_select_fusion
  254.9 251.2 %while.10 = (s32[]{:T(128)}, bf16[16,128,1,8,128]{4,3,1,0,2:T(8,128)(2,1)}, s32[16]{0:T(128)S(1)}, bf16[23,128,128]{2,1,0:T(8,128)(2,1)}, bf16[16,4,128,128]{3,2...) while((s32[]{:T(128)}, ...), condition=%wide.region_5.7_spmd, body=%wide.region_2.6_spmd.sunk | while | flops 826882048 | bytes 26014728 | solution.py:129
  266.5 1.5 fusion.41
  268.0 1.7 fusion.42
  282.2 1.5 fusion.41
  283.7 1.7 fusion.42
  297.9 1.5 fusion.41
  299.4 1.7 fusion.42
  313.6 1.5 fusion.41
  315.1 1.7 fusion.42
  329.3 1.5 fusion.41
  330.8 1.7 fusion.42
  346.5 1.7 fusion.42
  362.2 1.7 fusion.42
  377.9 1.7 fusion.42
  392.1 1.5 fusion.41
  393.6 1.7 fusion.42
  407.7 1.5 fusion.41
  409.3 1.7 fusion.42
  423.4 1.5 fusion.41
  425.0 1.7 fusion.42
  439.1 1.5 fusion.41
  440.7 1.7 fusion.42
  454.8 1.5 fusion.41
  456.4 1.7 fusion.42
  470.5 1.5 fusion.41
  472.1 1.7 fusion.42
  487.8 1.7 fusion.42
  503.5 1.7 fusion.42
  506.1 7.3 %all_to_all.63 = bf16[8,256,1024]{2,1,0:T(8,128)(2,1)} reshape(bf16[16,128,1,8,128]{4,3,1,0,2:T(8,128)(2,1)} %get-tuple-element.68) | data formatting | bytes 8388608 | tf_op jit(solution)/shard_map/all_to_all | solution.py:131
  513.4 54.1 %all_to_all.74 = bf16[8,256,1024]{2,1,0:T(8,128)(2,1)} all-to-all(bf16[8,256,1024]{2,1,0:T(8,128)(2,1)} %all_to_all.63), channel_id=1, replica_groups=mesh['ctx'=16,'head'=8] {'head'}, dimensions={0} | all-to-all | bytes 8388608 | tf_op jit(solution)/shard_map/all_to_all | solution.py:131
  567.6 6.5 %copy.41 = bf16[256,8,1024]{0,2,1:T(8,128)(2,1)} copy(bf16[256,8,1024]{2,0,1:T(8,128)(2,1)} %bitcast.167) | data formatting | bytes 8388608 | tf_op jit(solution)/shard_map/all_to_all | solution.py:131
  574.1 6.4 %copy.42 = bf16[256,8192]{1,0:T(8,128)(2,1)} copy(bf16[256,8192]{0,1:T(8,128)(2,1)} %bitcast.168) | data formatting | bytes 8388608 | tf_op jit(solution)/shard_map/all_to_all | solution.py:131
  (380 shorter events, 154.9 us)
Async XLA Ops:
  6.5 1.0 copy-start
  6.5 238.8 %all-gather.2.cloned.1.call-start = ((), (), s32[]{:S(2)}) async-start(), calls=%async_computation.5 | async-start | bytes 8912896 | tf_op jit(solution)/shard_map/all_gather | solution.py:93
  24.2 13.7 %all-to-all-start.1 = ((bf16[256,8,128]{2,0,1:T(8,128)(2,1)}), bf16[256,8,128]{2,0,1:T(8,128)(2,1)S(1)}, u32[]{:S(2)}, u32[]{:S(2)}) async-start(bf16[256,8,128]{2,0,1:T(8,128)(2,1)} %copy_bitcast_fusion.3), calls=%async_computation.1 | async-start | bytes 1048576 | tf_op jit(solution)/shard_map/all_to_all | solution.py:70
  97.5 8.3 %copy-start.4 = (s32[256,4]{0,1:T(4,128)S(1)}, s32[256,4]{0,1:T(4,128)}, u32[]{:S(2)}) copy-start(s32[256,4]{0,1:T(4,128)} %param.15) | copy-start | bytes 12292
  97.5 8.3 %copy-start.5 = (s32[256,4]{0,1:T(4,128)S(1)}, s32[256,4]{0,1:T(4,128)}, u32[]{:S(2)}) copy-start(s32[256,4]{0,1:T(4,128)} %param.14) | copy-start | bytes 12292
  97.5 8.7 %copy-start.3 = (s32[256]{0:T(256)S(1)}, s32[256]{0:T(256)}, u32[]{:S(2)}) copy-start(s32[256]{0:T(256)} %param.13) | copy-start | bytes 3076
  97.5 9.6 %copy-start.2 = (bf16[256,8,128]{2,0,1:T(8,128)(2,1)S(1)}, bf16[256,8,128]{2,0,1:T(8,128)(2,1)}, u32[]{:S(2)}) copy-start(bf16[256,8,128]{2,0,1:T(8,128)(2,1)} %all_to_all.72) | copy-start | bytes 1572868
  97.5 143.5 %all-to-all-start.2 = ((bf16[16,16,128,128]{3,2,1,0:T(8,128)(2,1)}), bf16[16,16,128,128]{3,2,1,0:T(8,128)(2,1)}, u32[]{:S(2)}, u32[]{:S(2)}) async-start(bf16[16,16,128,128]{3,2,1,0:T(8,128)(2,1)} %stack.3), calls=%async_computation.2 | async-start | bytes 16777216 | tf_op jit(solution)/shard_map/all_to_all | solution.py:65
  107.1 125.4 %collective-permute-start = (bf16[7,128,128]{2,1,0:T(8,128)(2,1)S(1)}, bf16[7,128,128]{2,1,0:T(8,128)(2,1)S(1)}, u32[]{:S(2)}, u32[]{:S(2)}) collective-permute-start(bf16[7,128,128]{2,1,0:T(8,128)(2,1)S(1)} %slice.32), channel_id=1, source_target_pairs={{0,8},{8,16},{16,24},{24,32},{32,40},{40,48},{48,56},{56,64},{64,7... | collective-permute-start | bytes 688136 | tf_op jit(solution)/shard_map/ppermute | solution.py:15
  110.5 125.2 %collective-permute-start.1 = (bf16[7,128,128]{2,1,0:T(8,128)(2,1)S(1)}, bf16[7,128,128]{2,1,0:T(8,128)(2,1)S(1)}, u32[]{:S(2)}, u32[]{:S(2)}) collective-permute-start(bf16[7,128,128]{2,1,0:T(8,128)(2,1)S(1)} %slice.33), channel_id=1, source_target_pairs={{0,8},{8,16},{16,24},{24,32},{32,40},{40,48},{48,56},{56,64},{64,7... | collective-permute-start | bytes 688136 | tf_op jit(solution)/shard_map/ppermute | solution.py:15
  574.1 6.4 %copy-start.1 = (bf16[256,1024]{1,0:T(8,128)(2,1)S(1)}, bf16[256,1024]{1,0:T(8,128)(2,1)}, u32[]{:S(2)}) copy-start(bf16[256,1024]{1,0:T(8,128)(2,1)} %param.12) | copy-start | bytes 1572868
Sparse Core Ops, SparseCore 0:
  22.4 71.1 all-gather.1
